TPU v7x, 32 devices: a whole 2x2x4 slice. The times are simulated.
32 devices in a mesh: seq: 4 (over y, x), shard: 8 (over z, core).
Axes of the slice: x: 2, y: 2, z: 4, core: 2. Of those that a mesh axis runs over, the one named last changes fastest.
Arguments:
- layer_in: bfloat16 [32, 1024, 768], P('shard', 'seq'), may hold values from -6 to 6
- layer_cotangent: bfloat16 [32, 1024, 768], P('shard', 'seq'), may hold values from -6 to 6
- doc_starts: int32 [32, 17], P('shard'), may hold values from 0 to 1024, as said below
- query_weight: float32 [768, 768], P(('seq', 'shard')), may hold values from -0.21875 to 0.21875
- key_weight: float32 [768, 768], P(('seq', 'shard')), may hold values from -0.21875 to 0.21875
- value_weight: float32 [768, 768], P(('seq', 'shard')), may hold values from -0.21875 to 0.21875
- out_weight: float32 [768, 768], P(('seq', 'shard')), may hold values from -3.5 to 3.5
- up_weight: float32 [768, 3072], P(('seq', 'shard')), may hold values from -0.21875 to 0.21875
- down_weight: float32 [3072, 768], P(('seq', 'shard')), may hold values from -0.109375 to 0.109375
- query_bias: float32 [768], P(('seq', 'shard')), may hold values from -0.625 to 0.625
- value_bias: float32 [768], P(('seq', 'shard')), may hold values from -0.1875 to 0.1875
- out_bias: float32 [768], P(('seq', 'shard')), may hold values from -0.625 to 0.625
- up_bias: float32 [3072], P(('seq', 'shard')), may hold values from -0.625 to 0.625
- down_bias: float32 [768], P(('seq', 'shard')), may hold values from -0.625 to 0.625
- mixer_gain: float32 [768], P(('seq', 'shard')), may hold values from 0.5 to 1.5
- mixer_shift: float32 [768], P(('seq', 'shard')), may hold values from -0.625 to 0.625
- final_gain: float32 [768], P(('seq', 'shard')), may hold values from 0.5 to 1.5
- final_shift: float32 [768], P(('seq', 'shard')), may hold values from -0.625 to 0.625
Outputs:
- layer_out: bfloat16 [32, 1024, 768], P('shard', 'seq')
- input_grad: float32 [32, 1024, 768], P('shard', 'seq')
- grad_query_weight: float32 [768, 768], P(('seq', 'shard'))
- grad_key_weight: float32 [768, 768], P(('seq', 'shard'))
- grad_value_weight: float32 [768, 768], P(('seq', 'shard'))
- grad_out_weight: float32 [768, 768], P(('seq', 'shard'))
- grad_up_weight: float32 [768, 3072], P(('seq', 'shard'))
- grad_down_weight: float32 [3072, 768], P(('seq', 'shard'))
- grad_query_bias: float32 [768], P(('seq', 'shard'))
- grad_value_bias: float32 [768], P(('seq', 'shard'))
- grad_out_bias: float32 [768], P(('seq', 'shard'))
- grad_up_bias: float32 [3072], P(('seq', 'shard'))
- grad_down_bias: float32 [768], P(('seq', 'shard'))
- grad_mixer_gain: float32 [768], P(('seq', 'shard'))
- grad_mixer_shift: float32 [768], P(('seq', 'shard'))
- grad_final_gain: float32 [768], P(('seq', 'shard'))
- grad_final_shift: float32 [768], P(('seq', 'shard'))
Inputs may be any that keep to these rules, and one draw needn't show every extreme that they name: `doc_starts`: each row lists the first positions of the documents of its stream in rising order; it begins with 0, entries equal to 1024 mark unused slots, and the last entry is always 1024. A document spans at most 512 positions, some document of every stream exactly that; every document but the last of a stream spans at least 64.
All inputs are finite; a program needn't handle non-finite values.
Results may differ from a plain program's by a relative error of at most 0.017.
Values may be sent and summed in bfloat16 or wider, within the bound.
No kernel may reach another device: no remote copies, remote signals or barrier semaphores. Data moves between devices by JAX's collectives and lax.ppermute only.
A program may use at most 192 MiB of HBM per device.

v0:
```python
import jax
import jax.numpy as jnp
from jax import lax
from jax.sharding import PartitionSpec as P

DH = 64
LEN = 1024
EPS = 1e-06
NEG = -1e30
ROOT_HALF = 0.7071067811865476
INV_ROOT_TWO_PI = 0.3989422804014327


def contract_rows(left, right):
    return lax.dot_general(
        left, right, (((0,), (0,)), ((), ())), preferred_element_type=jnp.float32
    )


def times_transpose(left, right):
    return lax.dot_general(
        left, right, (((1,), (1,)), ((), ())), preferred_element_type=jnp.float32
    )


def segment_ids(starts, length):
    places = lax.broadcasted_iota(jnp.int32, (1, length, 1), 1)
    return jnp.sum((starts[:, None, :] <= places).astype(jnp.int32), axis=2)


def norm_forward(rows, gain, shift):
    middle = jnp.mean(rows, axis=-1, keepdims=True)
    centred = rows - middle
    spread = jnp.mean(centred * centred, axis=-1, keepdims=True)
    inverse = lax.rsqrt(spread + EPS)
    normed = centred * inverse
    return (normed * gain + shift, normed, inverse)


def norm_backward(upstream, gain, normed, inverse):
    scaled = upstream * gain
    inner = jnp.mean(scaled, axis=-1, keepdims=True)
    along = jnp.mean(scaled * normed, axis=-1, keepdims=True)
    return inverse * (scaled - inner - normed * along)


def gelu_value(value):
    return 0.5 * value * (1.0 + lax.erf(value * ROOT_HALF))


def gelu_slope(value):
    return (
        0.5 * (1.0 + lax.erf(value * ROOT_HALF))
        + value * jnp.exp(-0.5 * value * value) * INV_ROOT_TWO_PI
    )


def masked_scores(queries, keys, seg_rows, seg_all, scale):
    scores = jnp.einsum("qhd,khd->hqk", queries, keys, preferred_element_type=jnp.float32) * scale
    allowed = seg_rows[:, None] == seg_all[None, :]
    return jnp.where(allowed[None], scores, NEG)


def attend_forward(item):
    queries, keys, values, segment = item
    length, heads, depth = queries.shape
    rows = min(512, length)
    blocks = length // rows
    scale = depth ** (-0.5)

    def one(piece):
        block_q, block_seg = piece
        scores = masked_scores(block_q, keys, block_seg, segment, scale)
        highest = jnp.max(scores, axis=-1, keepdims=True)
        raised = jnp.exp(scores - highest)
        total = jnp.sum(raised, axis=-1, keepdims=True)
        weights = (raised / total).astype(jnp.bfloat16)
        context = jnp.einsum("hqk,khd->qhd", weights, values, preferred_element_type=jnp.float32)
        return (context.astype(jnp.bfloat16), (highest + jnp.log(total))[..., 0])

    context, logsum = lax.map(
        one, (queries.reshape(blocks, rows, heads, depth), segment.reshape(blocks, rows))
    )
    return (context.reshape(length, heads, depth), logsum)


def attend_backward(item):
    queries, keys, values, segment, logsum, upstream = item
    length, heads, depth = queries.shape
    rows = min(512, length)
    blocks = length // rows
    scale = depth ** (-0.5)

    def one(carry, piece):
        key_acc, value_acc = carry
        block_q, block_seg, block_sum, block_up = piece
        scores = masked_scores(block_q, keys, block_seg, segment, scale)
        weights = jnp.exp(scores - block_sum[..., None])
        value_acc = value_acc + jnp.einsum(
            "hqk,qhd->khd",
            weights.astype(jnp.bfloat16),
            block_up,
            preferred_element_type=jnp.float32,
        )
        slope = jnp.einsum("qhd,khd->hqk", block_up, values, preferred_element_type=jnp.float32)
        inner = jnp.sum(weights * slope, axis=-1, keepdims=True)
        score_grad = (weights * (slope - inner)).astype(jnp.bfloat16)
        query_grad = (
            jnp.einsum("hqk,khd->qhd", score_grad, keys, preferred_element_type=jnp.float32) * scale
        )
        key_acc = (
            key_acc
            + jnp.einsum("hqk,qhd->khd", score_grad, block_q, preferred_element_type=jnp.float32)
            * scale
        )
        return ((key_acc, value_acc), query_grad.astype(jnp.bfloat16))

    empty = jnp.zeros((length, heads, depth), jnp.float32)
    pieces = (
        queries.reshape(blocks, rows, heads, depth),
        segment.reshape(blocks, rows),
        logsum,
        upstream.reshape(blocks, rows, heads, depth),
    )
    (key_grad, value_grad), query_grad = lax.scan(one, (empty, empty), pieces)
    return (
        query_grad.reshape(length, heads, depth),
        key_grad.astype(jnp.bfloat16),
        value_grad.astype(jnp.bfloat16),
    )


def per_device(
    layer_in,
    layer_cotangent,
    doc_starts,
    query_weight,
    key_weight,
    value_weight,
    out_weight,
    up_weight,
    down_weight,
    query_bias,
    value_bias,
    out_bias,
    up_bias,
    down_bias,
    mixer_gain,
    mixer_shift,
    final_gain,
    final_shift,
):
    (
        full_query,
        full_key,
        full_value,
        full_out,
        full_up,
        full_down,
        bias_query,
        bias_value,
        bias_out,
        bias_up,
        bias_down,
        gain_mixer,
        shift_mixer,
        gain_final,
        shift_final,
    ) = (
        lax.all_gather(query_weight.astype(jnp.bfloat16), ("seq", "shard"), axis=0, tiled=True),
        lax.all_gather(key_weight.astype(jnp.bfloat16), ("seq", "shard"), axis=0, tiled=True),
        lax.all_gather(value_weight.astype(jnp.bfloat16), ("seq", "shard"), axis=0, tiled=True),
        lax.all_gather(out_weight.astype(jnp.bfloat16), ("seq", "shard"), axis=0, tiled=True),
        lax.all_gather(up_weight.astype(jnp.bfloat16), ("seq", "shard"), axis=0, tiled=True),
        lax.all_gather(down_weight.astype(jnp.bfloat16), ("seq", "shard"), axis=0, tiled=True),
        lax.all_gather(query_bias.astype(jnp.bfloat16), ("seq", "shard"), axis=0, tiled=True),
        lax.all_gather(value_bias.astype(jnp.bfloat16), ("seq", "shard"), axis=0, tiled=True),
        lax.all_gather(out_bias.astype(jnp.bfloat16), ("seq", "shard"), axis=0, tiled=True),
        lax.all_gather(up_bias.astype(jnp.bfloat16), ("seq", "shard"), axis=0, tiled=True),
        lax.all_gather(down_bias.astype(jnp.bfloat16), ("seq", "shard"), axis=0, tiled=True),
        lax.all_gather(mixer_gain.astype(jnp.bfloat16), ("seq", "shard"), axis=0, tiled=True),
        lax.all_gather(mixer_shift.astype(jnp.bfloat16), ("seq", "shard"), axis=0, tiled=True),
        lax.all_gather(final_gain.astype(jnp.bfloat16), ("seq", "shard"), axis=0, tiled=True),
        lax.all_gather(final_shift.astype(jnp.bfloat16), ("seq", "shard"), axis=0, tiled=True),
    )
    local_in, local_up = (layer_in, layer_cotangent)
    streams, part_len, width = local_in.shape
    row_count = streams * part_len
    heads = width // DH
    flat = local_in.reshape(row_count, width)
    split_shape = (streams, part_len, heads, DH)
    queries = (
        jnp.dot(flat, full_query, preferred_element_type=jnp.float32)
        + bias_query.astype(jnp.float32)
    ).astype(jnp.bfloat16)
    keys = jnp.dot(flat, full_key, preferred_element_type=jnp.float32).astype(jnp.bfloat16)
    values = (
        jnp.dot(flat, full_value, preferred_element_type=jnp.float32)
        + bias_value.astype(jnp.float32)
    ).astype(jnp.bfloat16)
    head_queries, head_keys, head_values = (
        lax.all_to_all(
            queries.reshape(split_shape), "seq", split_axis=2, concat_axis=1, tiled=True
        ),
        lax.all_to_all(keys.reshape(split_shape), "seq", split_axis=2, concat_axis=1, tiled=True),
        lax.all_to_all(values.reshape(split_shape), "seq", split_axis=2, concat_axis=1, tiled=True),
    )
    segment = segment_ids(doc_starts, LEN)
    context, logsum = lax.map(attend_forward, (head_queries, head_keys, head_values, segment))
    context_rows = lax.all_to_all(context, "seq", split_axis=1, concat_axis=2, tiled=True).reshape(
        row_count, width
    )
    attn = jnp.dot(context_rows, full_out, preferred_element_type=jnp.float32) + bias_out.astype(
        jnp.float32
    )
    mixed, normed_mixer, inverse_mixer = norm_forward(
        flat.astype(jnp.float32) + attn,
        gain_mixer.astype(jnp.float32),
        shift_mixer.astype(jnp.float32),
    )
    upper = mixed.astype(jnp.bfloat16)
    preact = jnp.dot(upper, full_up, preferred_element_type=jnp.float32) + bias_up.astype(
        jnp.float32
    )
    hidden = gelu_value(preact).astype(jnp.bfloat16)
    ffout = jnp.dot(hidden, full_down, preferred_element_type=jnp.float32) + bias_down.astype(
        jnp.float32
    )
    result, normed_final, inverse_final = norm_forward(
        mixed + ffout, gain_final.astype(jnp.float32), shift_final.astype(jnp.float32)
    )
    layer_out = result.astype(jnp.bfloat16).reshape(streams, part_len, width)
    upstream = local_up.reshape(row_count, width).astype(jnp.float32)
    grad_final_gain = jnp.sum(upstream * normed_final, axis=0)
    grad_final_shift = jnp.sum(upstream, axis=0)
    back_final = norm_backward(
        upstream, gain_final.astype(jnp.float32), normed_final, inverse_final
    )
    back_ffout = back_final.astype(jnp.bfloat16)
    grad_down_weight = contract_rows(hidden, back_ffout)
    grad_down_bias = jnp.sum(back_ffout.astype(jnp.float32), axis=0)
    back_preact = (times_transpose(back_ffout, full_down) * gelu_slope(preact)).astype(jnp.bfloat16)
    grad_up_weight = contract_rows(upper, back_preact)
    grad_up_bias = jnp.sum(back_preact.astype(jnp.float32), axis=0)
    back_mixed = back_final + times_transpose(back_preact, full_up)
    grad_mixer_gain = jnp.sum(back_mixed * normed_mixer, axis=0)
    grad_mixer_shift = jnp.sum(back_mixed, axis=0)
    back_first = norm_backward(
        back_mixed, gain_mixer.astype(jnp.float32), normed_mixer, inverse_mixer
    )
    back_attn = back_first.astype(jnp.bfloat16)
    grad_out_weight = contract_rows(context_rows, back_attn)
    grad_out_bias = jnp.sum(back_attn.astype(jnp.float32), axis=0)
    back_context = times_transpose(back_attn, full_out).astype(jnp.bfloat16)
    head_back = lax.all_to_all(
        back_context.reshape(split_shape), "seq", split_axis=2, concat_axis=1, tiled=True
    )
    query_back, key_back, value_back = lax.map(
        attend_backward, (head_queries, head_keys, head_values, segment, logsum, head_back)
    )
    query_rows, key_rows, value_rows = (
        lax.all_to_all(query_back, "seq", split_axis=1, concat_axis=2, tiled=True),
        lax.all_to_all(key_back, "seq", split_axis=1, concat_axis=2, tiled=True),
        lax.all_to_all(value_back, "seq", split_axis=1, concat_axis=2, tiled=True),
    )
    query_rows = query_rows.reshape(row_count, width)
    key_rows = key_rows.reshape(row_count, width)
    value_rows = value_rows.reshape(row_count, width)
    grad_query_weight = contract_rows(flat, query_rows)
    grad_key_weight = contract_rows(flat, key_rows)
    grad_value_weight = contract_rows(flat, value_rows)
    grad_query_bias = jnp.sum(query_rows.astype(jnp.float32), axis=0)
    grad_value_bias = jnp.sum(value_rows.astype(jnp.float32), axis=0)
    input_grad = (
        back_first
        + times_transpose(query_rows, full_query)
        + times_transpose(key_rows, full_key)
        + times_transpose(value_rows, full_value)
    ).reshape(streams, part_len, width)
    (
        sum_query_weight,
        sum_key_weight,
        sum_value_weight,
        sum_out_weight,
        sum_up_weight,
        sum_down_weight,
        sum_query_bias,
        sum_value_bias,
        sum_out_bias,
        sum_up_bias,
        sum_down_bias,
        sum_mixer_gain,
        sum_mixer_shift,
        sum_final_gain,
        sum_final_shift,
    ) = (
        lax.psum_scatter(grad_query_weight, ("seq", "shard"), scatter_dimension=0, tiled=True),
        lax.psum_scatter(grad_key_weight, ("seq", "shard"), scatter_dimension=0, tiled=True),
        lax.psum_scatter(grad_value_weight, ("seq", "shard"), scatter_dimension=0, tiled=True),
        lax.psum_scatter(grad_out_weight, ("seq", "shard"), scatter_dimension=0, tiled=True),
        lax.psum_scatter(grad_up_weight, ("seq", "shard"), scatter_dimension=0, tiled=True),
        lax.psum_scatter(grad_down_weight, ("seq", "shard"), scatter_dimension=0, tiled=True),
        lax.psum_scatter(grad_query_bias, ("seq", "shard"), scatter_dimension=0, tiled=True),
        lax.psum_scatter(grad_value_bias, ("seq", "shard"), scatter_dimension=0, tiled=True),
        lax.psum_scatter(grad_out_bias, ("seq", "shard"), scatter_dimension=0, tiled=True),
        lax.psum_scatter(grad_up_bias, ("seq", "shard"), scatter_dimension=0, tiled=True),
        lax.psum_scatter(grad_down_bias, ("seq", "shard"), scatter_dimension=0, tiled=True),
        lax.psum_scatter(grad_mixer_gain, ("seq", "shard"), scatter_dimension=0, tiled=True),
        lax.psum_scatter(grad_mixer_shift, ("seq", "shard"), scatter_dimension=0, tiled=True),
        lax.psum_scatter(grad_final_gain, ("seq", "shard"), scatter_dimension=0, tiled=True),
        lax.psum_scatter(grad_final_shift, ("seq", "shard"), scatter_dimension=0, tiled=True),
    )
    return (
        layer_out,
        input_grad,
        sum_query_weight,
        sum_key_weight,
        sum_value_weight,
        sum_out_weight,
        sum_up_weight,
        sum_down_weight,
        sum_query_bias,
        sum_value_bias,
        sum_out_bias,
        sum_up_bias,
        sum_down_bias,
        sum_mixer_gain,
        sum_mixer_shift,
        sum_final_gain,
        sum_final_shift,
    )


def solution(mesh):
    in_specs = (
        P("shard", "seq", None),
        P("shard", "seq", None),
        P("shard", None),
        P(("seq", "shard"), None),
        P(("seq", "shard"), None),
        P(("seq", "shard"), None),
        P(("seq", "shard"), None),
        P(("seq", "shard"), None),
        P(("seq", "shard"), None),
        P(("seq", "shard")),
        P(("seq", "shard")),
        P(("seq", "shard")),
        P(("seq", "shard")),
        P(("seq", "shard")),
        P(("seq", "shard")),
        P(("seq", "shard")),
        P(("seq", "shard")),
        P(("seq", "shard")),
    )
    out_specs = (
        P("shard", "seq", None),
        P("shard", "seq", None),
        P(("seq", "shard"), None),
        P(("seq", "shard"), None),
        P(("seq", "shard"), None),
        P(("seq", "shard"), None),
        P(("seq", "shard"), None),
        P(("seq", "shard"), None),
        P(("seq", "shard")),
        P(("seq", "shard")),
        P(("seq", "shard")),
        P(("seq", "shard")),
        P(("seq", "shard")),
        P(("seq", "shard")),
        P(("seq", "shard")),
        P(("seq", "shard")),
        P(("seq", "shard")),
    )
    return jax.shard_map(
        per_device, mesh=mesh, in_specs=in_specs, out_specs=out_specs, check_vma=False
    )
```

profile of v0, /device:TPU:0, one launch (start us, length us, event | category | flops | bytes accessed | tf_op | source)
XLA Modules:
  0.0 1251.4 jit_solution(2350865984096955184)
XLA Ops:
  23.0 42.7 %all-reduce.19 = (bf16[768]{0:T(1024)(128)(2,1)S(1)}, bf16[768]{0:T(1024)(128)(2,1)S(1)}, bf16[768]{0:T(1024)(128)(2,1)}, bf16[768]{0:T(1024)(128)(2,1)}, bf16[7...) all-reduce(bf16[768]{0:T(1024)(128)(2,1)S(1)} %dynamic-update-slice, ...), channel_id=1, replica_groups=mesh['seq'=4,'shard'=8] {'seq','shard'}, use_global_device_ids=true, to_apply=%add | all-reduce | flops 9216 | bytes 36864
  68.5 3.1 add_convert_fusion.1
  74.7 3.6 all-to-all-start.2
  78.3 52.2 %all-gather.7.cloned.1.call-done = bf16[768,768]{1,0:T(8,128)(2,1)} async-done(((bf16[24,768]{1,0:T(8,128)(2,1)}), bf16[768,768]{1,0:T(8,128)(2,1)}) %all-gather.7.cloned.1.call-update) | async-done | bytes 1179664 | tf_op jit(solution)/shard_map/all_gather | solution.py:170
  130.6 4.3 add_convert_fusion.2
  138.9 3.6 all-to-all-start
  142.5 49.7 %all-gather.9.cloned.1.call-done = bf16[768,768]{1,0:T(8,128)(2,1)} async-done(((bf16[24,768]{1,0:T(8,128)(2,1)}), bf16[768,768]{1,0:T(8,128)(2,1)}) %all-gather.9.cloned.1.call-update) | async-done | bytes 1179664 | tf_op jit(solution)/shard_map/all_gather | solution.py:171
  192.2 4.3 convolution_convert_fusion.1
  199.1 3.9 reshape.248
  203.0 4.3 all-to-all-start.1
  211.3 17.1 %all-to-all-done.1 = bf16[4,256,12,64]{1,0,3,2:T(4,128)(2,1)} async-done(((bf16[4,256,12,64]{1,0,3,2:T(4,128)(2,1)}), bf16[4,256,12,64]{1,0,3,2:T(4,128)(2,1)}, u32[]{:S(2)}, u32[]{:S(2)}) %all-to-all-start.1) | async-done | bytes 1572896 | tf_op jit(solution)/shard_map/all_to_all | solution.py:205
  231.4 3.1 broadcast.164.clone.1
  234.5 70.0 %while.54 = (s32[]{:T(128)}, bf16[4,1024,3,64]{3,2,1,0:T(4,128)(2,1)}, f32[4,2,3,512]{3,2,1,0:T(4,128)}, bf16[4,1024,3,64]{1,3,2,0:T(8,128)(2,1)S(1)}, s32[4,102...) while((s32[]{:T(128)}, ...), condition=%wide.region_6.7_spmd, body=%wide.region_1.6_spmd.sunk | while | flops 422148608 | bytes 28430672 | solution.py:209
  238.0 11.3 while.57
  255.5 11.3 while.57
  273.0 11.3 while.57
  290.5 11.3 while.57
  304.5 8.5 copy.203
  313.1 5.2 reshape.300
  318.2 4.7 all-to-all-start.3
  324.4 18.5 %all-to-all-done.3 = bf16[4,2,98304]{2,1,0:T(2,128)(2,1)} async-done(((bf16[4,2,98304]{2,1,0:T(2,128)(2,1)}), bf16[4,2,98304]{2,1,0:T(2,128)(2,1)}, u32[]{:S(2)}, u32[]{:S(2)}) %all-to-all-start.3) | async-done | bytes 1572896 | tf_op jit(solution)/shard_map/all_to_all | solution.py:210
  342.9 3.8 reshape.301
  346.7 3.8 copy.170
  353.5 3.9 fusion.70
  357.9 12.8 %multiply_convert_fusion.1 = (bf16[1024,3072]{1,0:T(8,128)(2,1)}, f32[1024,3072]{1,0:T(8,128)}) fusion(f32[3072]{0:T(1024)S(1)} %convert_element_type.186, bf16[768,3072]{1,0:T(8,128)(2,1)} %all-gather.15.cloned.1.call-done, f32[1024,768]{1,0:T(8,128)S(1)} %get-tuple-element.625, f32[768]{0:T(1024)S(1)} %convert_element_type.182, ...), kind=kOutput, calls=%fused_computation.75 | convolution fusion | flops 4854644736 | bytes 26765312 | tf_op jit(solution)/shard_map/dot_general | solution.py:222
  370.7 14.1 %all-gather.17.cloned.1.call-done = bf16[3072,768]{1,0:T(8,128)(2,1)} async-done(((bf16[96,768]{1,0:T(8,128)(2,1)}), bf16[3072,768]{1,0:T(8,128)(2,1)}) %all-gather.17.cloned.1.call-update) | async-done | bytes 4718608 | tf_op jit(solution)/shard_map/all_gather | solution.py:175
  384.8 8.8 fusion.71
  399.7 14.1 %convert_reduce_fusion = (f32[3072]{0:T(1024)}, bf16[1024,3072]{1,0:T(8,128)(2,1)S(1)}) fusion(f32[1024,3072]{1,0:T(8,128)} %get-tuple-element.627, f32[3072]{0:T(1024)S(1)} %convert_element_type.186, bf16[3072,768]{1,0:T(8,128)(2,1)S(1)} %copy-done.46, f32[1024,768]{1,0:T(8,128)S(1)} %get-tuple-element.612), kind=kOutput, calls=%fused_computation.74 | convolution fusion | flops 4873516032 | bytes 26763264 | tf_op jit(solution)/shard_map/dot_general | solution.py:21
  413.8 6.5 multiply_reduce_fusion.1
  426.9 4.0 reshape.252
  430.9 4.4 all-to-all-start.4
  435.4 4.2 fusion.57
  439.7 15.6 %all-to-all-done.4 = bf16[4,256,12,64]{1,0,3,2:T(4,128)(2,1)} async-done(((bf16[4,256,12,64]{1,0,3,2:T(4,128)(2,1)}), bf16[4,256,12,64]{1,0,3,2:T(4,128)(2,1)}, u32[]{:S(2)}, u32[]{:S(2)}) %all-to-all-start.4) | async-done | bytes 1572896 | tf_op jit(solution)/shard_map/all_to_all | solution.py:255
  461.4 142.2 %while.56 = (s32[]{:T(128)}, bf16[4,1024,3,64]{3,2,1,0:T(4,128)(2,1)}, bf16[4,1024,3,64]{1,3,2,0:T(8,128)(2,1)}, bf16[4,1024,3,64]{1,3,2,0:T(8,128)(2,1)}, bf16[...) while((s32[]{:T(128)}, ...), condition=%wide.region_19.20_spmd, body=%wide.region_15.19_spmd.sunk | while | flops 1032321536 | bytes 67146216 | solution.py:258
  470.3 22.2 %while.58 = (s32[]{:T(128)}, f32[1024,3,64]{0,2,1:T(8,128)S(1)}, f32[1024,3,64]{0,2,1:T(8,128)S(1)}, bf16[2,512,3,64]{1,3,2,0:T(8,128)(2,1)S(1)}, bf16[2,512,3,6...) while((s32[]{:T(128)}, f32[1024,3,64]{0,2,1:T(8,128)S(1)}, ...), condition=%wide.region_18.18_spmd.clone, body=%wide.region_16.17_spmd.clone.sunk | while | flops 1031928320 | bytes 54649000 | solution.py:125
  505.8 22.2 %while.58 = (s32[]{:T(128)}, f32[1024,3,64]{0,2,1:T(8,128)S(1)}, f32[1024,3,64]{0,2,1:T(8,128)S(1)}, bf16[2,512,3,64]{1,3,2,0:T(8,128)(2,1)S(1)}, bf16[2,512,3,6...) while((s32[]{:T(128)}, f32[1024,3,64]{0,2,1:T(8,128)S(1)}, ...), condition=%wide.region_18.18_spmd.clone, body=%wide.region_16.17_spmd.clone.sunk | while | flops 1031928320 | bytes 54649000 | solution.py:125
  541.3 22.2 %while.58 = (s32[]{:T(128)}, f32[1024,3,64]{0,2,1:T(8,128)S(1)}, f32[1024,3,64]{0,2,1:T(8,128)S(1)}, bf16[2,512,3,64]{1,3,2,0:T(8,128)(2,1)S(1)}, bf16[2,512,3,6...) while((s32[]{:T(128)}, f32[1024,3,64]{0,2,1:T(8,128)S(1)}, ...), condition=%wide.region_18.18_spmd.clone, body=%wide.region_16.17_spmd.clone.sunk | while | flops 1031928320 | bytes 54649000 | solution.py:125
  576.8 22.2 %while.58 = (s32[]{:T(128)}, f32[1024,3,64]{0,2,1:T(8,128)S(1)}, f32[1024,3,64]{0,2,1:T(8,128)S(1)}, bf16[2,512,3,64]{1,3,2,0:T(8,128)(2,1)S(1)}, bf16[2,512,3,6...) while((s32[]{:T(128)}, f32[1024,3,64]{0,2,1:T(8,128)S(1)}, ...), condition=%wide.region_18.18_spmd.clone, body=%wide.region_16.17_spmd.clone.sunk | while | flops 1031928320 | bytes 54649000 | solution.py:125
  603.7 4.7 copy.180
  608.3 3.3 reshape.306
  611.7 23.3 %all_to_all.132 = bf16[4,2,98304]{2,1,0:T(2,128)(2,1)S(1)} all-to-all(bf16[4,2,98304]{2,1,0:T(2,128)(2,1)} %reshape.306), channel_id=1, replica_groups=mesh['seq'=4,'shard'=8] {'seq'}, dimensions={0} | all-to-all | bytes 3145728 | tf_op jit(solution)/shard_map/all_to_all | solution.py:264
  635.0 3.3 reshape.307
  638.3 4.9 copy.181
  647.7 3.2 copy.189
  650.9 6.2 copy.202
  657.2 3.3 reshape.304
  660.5 21.9 %all_to_all.133 = bf16[4,2,98304]{2,1,0:T(2,128)(2,1)S(1)} all-to-all(bf16[4,2,98304]{2,1,0:T(2,128)(2,1)} %reshape.304), channel_id=1, replica_groups=mesh['seq'=4,'shard'=8] {'seq'}, dimensions={0} | all-to-all | bytes 3145728 | tf_op jit(solution)/shard_map/all_to_all | solution.py:262
  682.4 3.3 reshape.305
  685.7 4.9 copy.177
  698.3 4.7 copy.178
  703.0 3.3 reshape.302
  706.3 23.6 %all_to_all.134 = bf16[4,2,98304]{2,1,0:T(2,128)(2,1)} all-to-all(bf16[4,2,98304]{2,1,0:T(2,128)(2,1)} %reshape.302), channel_id=1, replica_groups=mesh['seq'=4,'shard'=8] {'seq'}, dimensions={0} | all-to-all | bytes 3145728 | tf_op jit(solution)/shard_map/all_to_all | solution.py:263
  729.9 3.8 reshape.303
  733.7 3.9 copy.179
  743.4 3.2 copy.187
  746.7 10.7 fusion.63
  759.3 10.2 fusion.60
  774.7 40.4 %all-reduce.18 = (f32[768]{0:T(1024)S(1)}, f32[768]{0:T(1024)S(1)}, f32[768]{0:T(1024)S(1)}, f32[3072]{0:T(1024)S(1)}, f32[768]{0:T(1024)S(1)}, /*index=5*/f32[7...) all-reduce(f32[768]{0:T(1024)S(1)} %reduce_sum.194, ...), channel_id=8, replica_groups=mesh['seq'=4,'shard'=8] {'seq','shard'}, use_global_device_ids=true, to_apply=%region_27.28.clone | all-reduce | flops 9216 | bytes 73728
  820.3 3.3 fusion.72
  826.5 3.2 add_add_fusion
  829.7 27.2 %reduce-scatter.19.cloned.1.call-done = f32[24,768]{1,0:T(8,128)} async-done(((f32[768,768]{1,0:T(8,128)}), f32[24,768]{1,0:T(8,128)}) %reduce-scatter.19.cloned.1.call-update) | async-done | bytes 73744
  856.9 104.3 %reduce-scatter.21.cloned.1.call-done = f32[24,768]{1,0:T(8,128)} async-done(((f32[768,768]{1,0:T(8,128)}), f32[24,768]{1,0:T(8,128)}) %reduce-scatter.21.cloned.1.call-update) | async-done | bytes 73744
  961.2 141.7 %reduce-scatter.15.cloned.1.call-done = f32[24,3072]{1,0:T(8,128)} async-done(((f32[768,3072]{1,0:T(8,128)}), f32[24,3072]{1,0:T(8,128)}) %reduce-scatter.15.cloned.1.call-update) | async-done | bytes 294928 | tf_op jit(solution)/shard_map/reduce_scatter | solution.py:301
  1102.9 141.5 %reduce-scatter.17.cloned.1.call-done = f32[96,768]{1,0:T(8,128)} async-done(((f32[3072,768]{1,0:T(8,128)}), f32[96,768]{1,0:T(8,128)}) %reduce-scatter.17.cloned.1.call-update) | async-done | bytes 294928 | tf_op jit(solution)/shard_map/reduce_scatter | solution.py:302
  (485 shorter events, 302.7 us)
Async XLA Ops:
  7.2 61.3 %all-gather.11.cloned.1.call-start = ((), (), s32[]{:S(2)}) async-start(), calls=%async_computation.16 | async-start | bytes 1216512 | tf_op jit(solution)/shard_map/all_gather | solution.py:172
  8.8 121.8 %all-gather.7.cloned.1.call-start = ((), (), s32[]{:S(2)}) async-start(), calls=%async_computation.14 | async-start | bytes 1216512 | tf_op jit(solution)/shard_map/all_gather | solution.py:170
  10.3 181.8 %all-gather.9.cloned.1.call-start = ((), (), s32[]{:S(2)}) async-start(), calls=%async_computation.15 | async-start | bytes 1216512 | tf_op jit(solution)/shard_map/all_gather | solution.py:171
  11.9 341.5 %all-gather.13.cloned.1.call-start = ((), (), s32[]{:S(2)}) async-start(), calls=%async_computation.17 | async-start | bytes 1216512 | tf_op jit(solution)/shard_map/all_gather | solution.py:173
  13.5 344.4 %all-gather.15.cloned.1.call-start = ((), (), s32[]{:S(2)}) async-start(), calls=%async_computation.18 | async-start | bytes 4866048 | tf_op jit(solution)/shard_map/all_gather | solution.py:174
  74.7 64.2 %all-to-all-start.2 = ((bf16[4,256,12,64]{1,0,3,2:T(4,128)(2,1)}), bf16[4,256,12,64]{1,0,3,2:T(4,128)(2,1)S(1)}, u32[]{:S(2)}, u32[]{:S(2)}) async-start(bf16[4,256,12,64]{1,0,3,2:T(4,128)(2,1)} %reshape.249), calls=%async_computation.2 | async-start | bytes 3145728 | tf_op jit(solution)/shard_map/all_to_all | solution.py:206
  138.9 64.1 %all-to-all-start = ((bf16[4,256,12,64]{1,0,3,2:T(4,128)(2,1)}), bf16[4,256,12,64]{1,0,3,2:T(4,128)(2,1)S(1)}, u32[]{:S(2)}, u32[]{:S(2)}) async-start(bf16[4,256,12,64]{1,0,3,2:T(4,128)(2,1)} %reshape.247), calls=%async_computation | async-start | bytes 3145728 | tf_op jit(solution)/shard_map/all_to_all | solution.py:202
  199.1 8.5 copy-start.24
  199.1 9.2 copy-start.39
  203.0 25.4 %all-to-all-start.1 = ((bf16[4,256,12,64]{1,0,3,2:T(4,128)(2,1)}), bf16[4,256,12,64]{1,0,3,2:T(4,128)(2,1)}, u32[]{:S(2)}, u32[]{:S(2)}) async-start(bf16[4,256,12,64]{1,0,3,2:T(4,128)(2,1)} %reshape.248), calls=%async_computation.1 | async-start | bytes 3145728 | tf_op jit(solution)/shard_map/all_to_all | solution.py:205
  207.3 177.4 %all-gather.17.cloned.1.call-start = ((), (), s32[]{:S(2)}) async-start(), calls=%async_computation.19 | async-start | bytes 4866048 | tf_op jit(solution)/shard_map/all_gather | solution.py:175
  304.5 8.5 copy-start.2
  313.0 9.9 copy-start.45
  313.0 9.9 copy-start.44
  313.0 10.0 copy-start.43
  313.0 10.0 copy-start.42
  313.0 10.0 copy-start.41
  313.0 10.0 copy-start.40
  313.0 10.0 copy-start.3
  318.2 6.2 copy-start.36
  318.2 24.7 %all-to-all-start.3 = ((bf16[4,2,98304]{2,1,0:T(2,128)(2,1)}), bf16[4,2,98304]{2,1,0:T(2,128)(2,1)}, u32[]{:S(2)}, u32[]{:S(2)}) async-start(bf16[4,2,98304]{2,1,0:T(2,128)(2,1)} %reshape.300), calls=%async_computation.3 | async-start | bytes 3145728 | tf_op jit(solution)/shard_map/all_to_all | solution.py:210
  322.9 97.4 %copy-start.27 = (f32[768]{0:T(1024)}, f32[768]{0:T(1024)S(1)}, u32[]{:S(2)}) copy-start(f32[768]{0:T(1024)S(1)} %convert_element_type.180) | copy-start | bytes 9220
  323.0 61.8 %copy-start.29 = (f32[768]{0:T(1024)}, f32[768]{0:T(1024)S(1)}, u32[]{:S(2)}) copy-start(f32[768]{0:T(1024)S(1)} %convert_element_type.182) | copy-start | bytes 9220
  357.3 63.0 %copy-start = (f32[1024,768]{1,0:T(8,128)}, f32[1024,768]{1,0:T(8,128)S(1)}, u32[]{:S(2)}) copy-start(f32[1024,768]{1,0:T(8,128)S(1)} %get-tuple-element.625) | copy-start | bytes 9437188
  357.3 63.0 %copy-start.22 = (f32[1024]{0:T(1024)}, f32[1024]{0:T(1024)S(1)}, u32[]{:S(2)}) copy-start(f32[1024]{0:T(1024)S(1)} %broadcast_multiply_fusion.4) | copy-start | bytes 12292
  357.9 62.5 %copy-start.25 = (f32[1024]{0:T(1024)}, f32[1024]{0:T(1024)S(1)}, u32[]{:S(2)}) copy-start(f32[1024]{0:T(1024)S(1)} %add_rsqrt_fusion.1) | copy-start | bytes 12292
  396.8 2.9 copy-start.46
  396.8 17.0 %slice-start = ((s8[4718592]{0:T(1024)(128)(4,1)}), s8[4194304]{0:T(1024)(128)(4,1)S(1)}, s32[]{:S(2)}) async-start(s8[4718592]{0:T(1024)(128)(4,1)} %bitcast.311), calls=%async_computation.26 | async-start | bytes 8388608
  399.7 14.1 %copy-start.16 = (f32[1024,768]{1,0:T(8,128)}, f32[1024,768]{1,0:T(8,128)S(1)}, u32[]{:S(2)}) copy-start(f32[1024,768]{1,0:T(8,128)S(1)} %get-tuple-element.612) | copy-start | bytes 9437188
  399.7 14.1 %slice-start.1 = ((s8[4718592]{0:T(1024)(128)(4,1)}), s8[524288]{0:T(1024)(128)(4,1)S(1)}, s32[]{:S(2)}) async-start(s8[4718592]{0:T(1024)(128)(4,1)} %bitcast.311), calls=%async_computation.27 | async-start | bytes 1048576
  413.8 6.5 copy-start.13
  420.4 3.4 copy-start.51
  426.9 8.5 copy-start.10
  430.9 24.4 %all-to-all-start.4 = ((bf16[4,256,12,64]{1,0,3,2:T(4,128)(2,1)}), bf16[4,256,12,64]{1,0,3,2:T(4,128)(2,1)}, u32[]{:S(2)}, u32[]{:S(2)}) async-start(bf16[4,256,12,64]{1,0,3,2:T(4,128)(2,1)} %reshape.252), calls=%async_computation.4 | async-start | bytes 3145728 | tf_op jit(solution)/shard_map/all_to_all | solution.py:255
  435.3 394.4 %reduce-scatter.13.cloned.1.call-start = ((), (), s32[]{:S(2)}) async-start(), calls=%async_computation.20 | async-start | bytes 2433024 | tf_op jit(solution)/shard_map/reduce_scatter | solution.py:300
  439.6 390.1 %reduce-scatter.23.cloned.1.call-start = ((), (), s32[]{:S(2)}) async-start(), calls=%async_computation.25 | async-start | bytes 2433024
  638.3 6.6 copy-start.47
  643.2 4.5 copy-start.5
  650.9 206.0 %reduce-scatter.19.cloned.1.call-start = ((), (), s32[]{:S(2)}) async-start(), calls=%async_computation.23 | async-start | bytes 2433024
  685.7 6.6 copy-start.48
  690.6 4.5 copy-start.7
  698.2 263.0 %reduce-scatter.21.cloned.1.call-start = ((), (), s32[]{:S(2)}) async-start(), calls=%async_computation.24 | async-start | bytes 2433024
  737.5 3.0 copy-start.49
  743.4 3.3 copy-start.1
  743.4 3.3 copy-start.23
  743.4 3.3 copy-start.26
  743.4 3.3 copy-start.28
  743.4 3.3 copy-start.30
  746.6 356.3 %reduce-scatter.15.cloned.1.call-start = ((), (), s32[]{:S(2)}) async-start(), calls=%async_computation.21 | async-start | bytes 9732096 | tf_op jit(solution)/shard_map/reduce_scatter | solution.py:301
  757.4 1.9 copy-start.17
  757.5 486.9 %reduce-scatter.17.cloned.1.call-start = ((), (), s32[]{:S(2)}) async-start(), calls=%async_computation.22 | async-start | bytes 9732096 | tf_op jit(solution)/shard_map/reduce_scatter | solution.py:302
  769.5 3.3 copy-start.8
  769.5 5.1 copy-start.31
  769.5 5.1 copy-start.32
  769.5 5.1 copy-start.33
  769.5 5.1 copy-start.34
  769.6 5.1 copy-start.35
  769.6 5.1 copy-start.37
  769.6 5.1 copy-start.38
  820.3 3.4 copy-start.20
  820.3 3.4 copy-start.50
  823.7 1.9 copy-start.11
  823.7 2.5 copy-start.15
  823.7 2.8 copy-start.21
  (10 other events, 11.5 us)
Sparse Core Ops, SparseCore 0:
  11.6 56.8 all-gather.10
  72.0 58.4 all-gather.6
  134.2 57.9 all-gather.8
  195.6 53.8 all-gather.12
  252.9 62.5 all-gather.14
  318.9 65.7 all-gather.16
  442.0 99.3 reduce-scatter.12
  651.0 101.0 reduce-scatter.22
  758.0 98.8 reduce-scatter.18
  862.6 98.5 reduce-scatter.20
  967.7 135.1 reduce-scatter.14
  1109.2 135.0 reduce-scatter.16
where the time goes:
time: 1260 us; the launch traced here: 1250 us
  waiting for transfers between devices  585 us (46%)
  local copies, waits for them, and re-layouts  217 us (17%)
  matrix products  188 us (15%)
  blocking collectives  152 us (12%)
  other arithmetic  71.6 us (6%)
  starting transfers between devices  21.2 us (2%)
  between operations  15.3 us (1%)
    reduce_scatter x1, waiting for transfers between devices, per_device(): lax.psum_scatter(grad_up_weight, ('seq', 'shard'), scatter_dimension=0, t...  142 us
    reduce_scatter x1, waiting for transfers between devices, per_device(): lax.psum_scatter(grad_down_weight, ('seq', 'shard'), scatter_dimension=0,...  141 us
    unnamed x15, waiting for transfers between devices  132 us
    unnamed x2, blocking collectives  83.1 us
    unnamed x150, local copies, waits for them, and re-layouts  62.4 us
    all_gather x1, waiting for transfers between devices, per_device(): lax.all_gather(query_weight.astype(jnp.bfloat16), ('seq', 'shard'), axis=...  52.2 us
    all_gather x1, waiting for transfers between devices, per_device(): lax.all_gather(key_weight.astype(jnp.bfloat16), ('seq', 'shard'), axis=0,...  49.7 us
    dot_general x6, matrix products, contract_rows(): lax.dot_general(left, right, (((0,), (0,)), ((), ())), preferred_element_...  33.5 us
  transfers between devices with their start and end apart: 17, of which 11 were waited for; matrix products, arithmetic and copies ran while one was open for 33% of the time, Pallas kernels for 0%

commit v1 on v0

--- a/solution.py
+++ b/solution.py
@@ -260,7 +260,12 @@
     )
     query_rows, key_rows, value_rows = (
         lax.all_to_all(query_back, "seq", split_axis=1, concat_axis=2, tiled=True),
-        lax.all_to_all(key_back, "seq", split_axis=1, concat_axis=2, tiled=True),
+        jnp.concatenate(
+            lax.all_to_all(
+                jnp.stack(jnp.split(key_back, lax.axis_size("seq"), axis=1)), "seq", 0, 0
+            ),
+            axis=2,
+        ),
         lax.all_to_all(value_back, "seq", split_axis=1, concat_axis=2, tiled=True),
     )
     query_rows = query_rows.reshape(row_count, width)

time: 1260 us -> 1250 us (level)
  local copies, waits for them, and re-layouts: 217 us -> 201 us
    unnamed x150 -> x148, local copies, waits for them, and re-layouts: 62.4 us -> 52.6 us
  transfers between devices with their start and end apart: 17 -> 17, of which waited for: 11 -> 11; matrix products, arithmetic and copies ran while one was open for 33% -> 32% of each run, Pallas kernels for 0% -> 0%
where the time goes in v1:
time: 1250 us; the launch traced here: 1230 us
  waiting for transfers between devices  587 us (47%)
  local copies, waits for them, and re-layouts  201 us (16%)
  matrix products  187 us (15%)
  blocking collectives  150 us (12%)
  other arithmetic  71.9 us (6%)
  starting transfers between devices  21.2 us (2%)
  between operations  15.3 us (1%)
    reduce_scatter x1, waiting for transfers between devices, per_device(): lax.psum_scatter(grad_up_weight, ('seq', 'shard'), scatter_dimension=0, t...  142 us
    reduce_scatter x1, waiting for transfers between devices, per_device(): lax.psum_scatter(grad_down_weight, ('seq', 'shard'), scatter_dimension=0,...  141 us
    unnamed x15, waiting for transfers between devices  134 us
    unnamed x2, blocking collectives  82.8 us
    unnamed x148, local copies, waits for them, and re-layouts  52.6 us
    all_gather x1, waiting for transfers between devices, per_device(): lax.all_gather(query_weight.astype(jnp.bfloat16), ('seq', 'shard'), axis=...  52.2 us
    all_gather x1, waiting for transfers between devices, per_device(): lax.all_gather(key_weight.astype(jnp.bfloat16), ('seq', 'shard'), axis=0,...  49.7 us
    dot_general x6, matrix products, contract_rows(): lax.dot_general(left, right, (((0,), (0,)), ((), ())), preferred_element_...  32.2 us
  transfers between devices with their start and end apart: 17, of which 11 were waited for; matrix products, arithmetic and copies ran while one was open for 32% of the time, Pallas kernels for 0%

profile of v1, /device:TPU:0, one launch (start us, length us, event | category | flops | bytes accessed | tf_op | source)
XLA Modules:
  0.0 1234.3 jit_solution(17089423095850186009)
XLA Ops:
  23.0 42.7 %all-reduce.19 = (bf16[768]{0:T(1024)(128)(2,1)S(1)}, bf16[768]{0:T(1024)(128)(2,1)S(1)}, bf16[768]{0:T(1024)(128)(2,1)}, bf16[768]{0:T(1024)(128)(2,1)}, bf16[7...) all-reduce(bf16[768]{0:T(1024)(128)(2,1)S(1)} %dynamic-update-slice, ...), channel_id=1, replica_groups=mesh['seq'=4,'shard'=8] {'seq','shard'}, use_global_device_ids=true, to_apply=%add | all-reduce | flops 9216 | bytes 36864
  68.5 3.1 add_convert_fusion.1
  74.7 3.6 all-to-all-start.2
  78.3 52.2 %all-gather.7.cloned.1.call-done = bf16[768,768]{1,0:T(8,128)(2,1)} async-done(((bf16[24,768]{1,0:T(8,128)(2,1)}), bf16[768,768]{1,0:T(8,128)(2,1)}) %all-gather.7.cloned.1.call-update) | async-done | bytes 1179664 | tf_op jit(solution)/shard_map/all_gather | solution.py:170
  130.6 4.3 add_convert_fusion.2
  138.9 3.6 all-to-all-start
  142.5 49.7 %all-gather.9.cloned.1.call-done = bf16[768,768]{1,0:T(8,128)(2,1)} async-done(((bf16[24,768]{1,0:T(8,128)(2,1)}), bf16[768,768]{1,0:T(8,128)(2,1)}) %all-gather.9.cloned.1.call-update) | async-done | bytes 1179664 | tf_op jit(solution)/shard_map/all_gather | solution.py:171
  192.2 4.3 convolution_convert_fusion.1
  199.1 3.9 reshape.247
  203.0 4.3 all-to-all-start.1
  211.3 17.1 %all-to-all-done.1 = bf16[4,256,12,64]{1,0,3,2:T(4,128)(2,1)} async-done(((bf16[4,256,12,64]{1,0,3,2:T(4,128)(2,1)}), bf16[4,256,12,64]{1,0,3,2:T(4,128)(2,1)}, u32[]{:S(2)}, u32[]{:S(2)}) %all-to-all-start.1) | async-done | bytes 1572896 | tf_op jit(solution)/shard_map/all_to_all | solution.py:205
  231.4 3.1 broadcast.164.clone.1
  234.5 70.0 %while.54 = (s32[]{:T(128)}, bf16[4,1024,3,64]{3,2,1,0:T(4,128)(2,1)}, f32[4,2,3,512]{3,2,1,0:T(4,128)}, bf16[4,1024,3,64]{1,3,2,0:T(8,128)(2,1)S(1)}, s32[4,102...) while((s32[]{:T(128)}, ...), condition=%wide.region_6.7_spmd, body=%wide.region_1.6_spmd.sunk | while | flops 422148608 | bytes 28430672 | solution.py:209
  238.0 11.3 while.57
  255.5 11.3 while.57
  273.0 11.3 while.57
  290.5 11.3 while.57
  304.5 8.5 copy.200
  313.1 5.2 reshape.299
  318.3 4.7 all-to-all-start.3
  324.4 18.5 %all-to-all-done.3 = bf16[4,2,98304]{2,1,0:T(2,128)(2,1)} async-done(((bf16[4,2,98304]{2,1,0:T(2,128)(2,1)}), bf16[4,2,98304]{2,1,0:T(2,128)(2,1)}, u32[]{:S(2)}, u32[]{:S(2)}) %all-to-all-start.3) | async-done | bytes 1572896 | tf_op jit(solution)/shard_map/all_to_all | solution.py:210
  342.9 3.8 reshape.300
  346.6 3.8 copy.168
  350.5 3.0 copy.192
  353.5 3.9 fusion.70
  357.9 12.7 %multiply_convert_fusion.1 = (bf16[1024,3072]{1,0:T(8,128)(2,1)}, f32[1024,3072]{1,0:T(8,128)}) fusion(f32[3072]{0:T(1024)S(1)} %convert_element_type.186, bf16[768,3072]{1,0:T(8,128)(2,1)} %all-gather.15.cloned.1.call-done, f32[1024,768]{1,0:T(8,128)S(1)} %get-tuple-element.629, f32[768]{0:T(1024)S(1)} %convert_element_type.182, ...), kind=kOutput, calls=%fused_computation.75 | convolution fusion | flops 4854644736 | bytes 26765312 | tf_op jit(solution)/shard_map/dot_general | solution.py:222
  370.6 14.1 %all-gather.17.cloned.1.call-done = bf16[3072,768]{1,0:T(8,128)(2,1)} async-done(((bf16[96,768]{1,0:T(8,128)(2,1)}), bf16[3072,768]{1,0:T(8,128)(2,1)}) %all-gather.17.cloned.1.call-update) | async-done | bytes 4718608 | tf_op jit(solution)/shard_map/all_gather | solution.py:175
  384.8 8.8 fusion.71
  396.8 2.9 convert_reduce_fusion.2
  399.7 14.1 %convert_reduce_fusion = (f32[3072]{0:T(1024)}, bf16[1024,3072]{1,0:T(8,128)(2,1)S(1)}) fusion(f32[1024,3072]{1,0:T(8,128)} %get-tuple-element.631, f32[3072]{0:T(1024)S(1)} %convert_element_type.186, bf16[3072,768]{1,0:T(8,128)(2,1)S(1)} %copy-done.46, f32[1024,768]{1,0:T(8,128)S(1)} %get-tuple-element.612), kind=kOutput, calls=%fused_computation.74 | convolution fusion | flops 4873516032 | bytes 26763264 | tf_op jit(solution)/shard_map/dot_general | solution.py:21
  413.8 6.5 multiply_reduce_fusion.1
  426.9 4.0 reshape.251
  430.9 4.4 all-to-all-start.4
  435.3 4.2 fusion.57
  439.7 15.6 %all-to-all-done.4 = bf16[4,256,12,64]{1,0,3,2:T(4,128)(2,1)} async-done(((bf16[4,256,12,64]{1,0,3,2:T(4,128)(2,1)}), bf16[4,256,12,64]{1,0,3,2:T(4,128)(2,1)}, u32[]{:S(2)}, u32[]{:S(2)}) %all-to-all-start.4) | async-done | bytes 1572896 | tf_op jit(solution)/shard_map/all_to_all | solution.py:255
  458.4 3.0 broadcast.164
  461.4 142.2 %while.56 = (s32[]{:T(128)}, bf16[4,1024,3,64]{3,2,1,0:T(4,128)(2,1)}, bf16[4,1024,3,64]{1,3,2,0:T(8,128)(2,1)}, bf16[4,1024,3,64]{1,3,2,0:T(8,128)(2,1)}, bf16[...) while((s32[]{:T(128)}, ...), condition=%wide.region_19.20_spmd, body=%wide.region_15.19_spmd.sunk | while | flops 1032321536 | bytes 67146216 | solution.py:258
  470.2 22.2 %while.58 = (s32[]{:T(128)}, f32[1024,3,64]{0,2,1:T(8,128)S(1)}, f32[1024,3,64]{0,2,1:T(8,128)S(1)}, bf16[2,512,3,64]{1,3,2,0:T(8,128)(2,1)S(1)}, bf16[2,512,3,6...) while((s32[]{:T(128)}, f32[1024,3,64]{0,2,1:T(8,128)S(1)}, ...), condition=%wide.region_18.18_spmd.clone, body=%wide.region_16.17_spmd.clone.sunk | while | flops 1031928320 | bytes 54649000 | solution.py:125
  505.7 22.2 %while.58 = (s32[]{:T(128)}, f32[1024,3,64]{0,2,1:T(8,128)S(1)}, f32[1024,3,64]{0,2,1:T(8,128)S(1)}, bf16[2,512,3,64]{1,3,2,0:T(8,128)(2,1)S(1)}, bf16[2,512,3,6...) while((s32[]{:T(128)}, f32[1024,3,64]{0,2,1:T(8,128)S(1)}, ...), condition=%wide.region_18.18_spmd.clone, body=%wide.region_16.17_spmd.clone.sunk | while | flops 1031928320 | bytes 54649000 | solution.py:125
  541.3 22.1 %while.58 = (s32[]{:T(128)}, f32[1024,3,64]{0,2,1:T(8,128)S(1)}, f32[1024,3,64]{0,2,1:T(8,128)S(1)}, bf16[2,512,3,64]{1,3,2,0:T(8,128)(2,1)S(1)}, bf16[2,512,3,6...) while((s32[]{:T(128)}, f32[1024,3,64]{0,2,1:T(8,128)S(1)}, ...), condition=%wide.region_18.18_spmd.clone, body=%wide.region_16.17_spmd.clone.sunk | while | flops 1031928320 | bytes 54649000 | solution.py:125
  576.8 22.1 %while.58 = (s32[]{:T(128)}, f32[1024,3,64]{0,2,1:T(8,128)S(1)}, f32[1024,3,64]{0,2,1:T(8,128)S(1)}, bf16[2,512,3,64]{1,3,2,0:T(8,128)(2,1)S(1)}, bf16[2,512,3,6...) while((s32[]{:T(128)}, f32[1024,3,64]{0,2,1:T(8,128)S(1)}, ...), condition=%wide.region_18.18_spmd.clone, body=%wide.region_16.17_spmd.clone.sunk | while | flops 1031928320 | bytes 54649000 | solution.py:125
  605.4 22.3 %all_to_all.122 = bf16[4,4,256,3,64]{2,4,3,1,0:T(8,128)(2,1)S(1)} all-to-all(bf16[4,4,256,3,64]{2,4,3,1,0:T(8,128)(2,1)S(1)} %pad_maximum_fusion), channel_id=1, replica_groups=mesh['seq'=4,'shard'=8] {'seq'}, dimensions={0} | all-to-all | bytes 3145728 | tf_op jit(solution)/shard_map/all_to_all | solution.py:264
  633.9 4.7 copy.177
  638.6 3.3 reshape.303
  641.9 21.9 %all_to_all.123 = bf16[4,2,98304]{2,1,0:T(2,128)(2,1)S(1)} all-to-all(bf16[4,2,98304]{2,1,0:T(2,128)(2,1)} %reshape.303), channel_id=1, replica_groups=mesh['seq'=4,'shard'=8] {'seq'}, dimensions={0} | all-to-all | bytes 3145728 | tf_op jit(solution)/shard_map/all_to_all | solution.py:269
  663.8 3.3 reshape.304
  667.1 4.9 copy.178
  676.5 3.1 copy.186
  679.7 6.3 copy.199
  685.9 3.3 reshape.301
  689.2 22.6 %all_to_all.124 = bf16[4,2,98304]{2,1,0:T(2,128)(2,1)S(1)} all-to-all(bf16[4,2,98304]{2,1,0:T(2,128)(2,1)} %reshape.301), channel_id=1, replica_groups=mesh['seq'=4,'shard'=8] {'seq'}, dimensions={0} | all-to-all | bytes 3145728 | tf_op jit(solution)/shard_map/all_to_all | solution.py:262
  711.8 3.3 reshape.302
  715.2 4.9 copy.175
  721.7 2.8 convolution_bitcast_fusion.2
  724.5 3.2 copy.182
  727.8 10.7 fusion.63
  740.4 10.2 fusion.60
  755.8 40.1 %all-reduce.18 = (f32[768]{0:T(1024)S(1)}, f32[768]{0:T(1024)S(1)}, f32[768]{0:T(1024)S(1)}, f32[3072]{0:T(1024)S(1)}, f32[768]{0:T(1024)S(1)}, /*index=5*/f32[7...) all-reduce(f32[768]{0:T(1024)S(1)} %reduce_sum.194, ...), channel_id=8, replica_groups=mesh['seq'=4,'shard'=8] {'seq','shard'}, use_global_device_ids=true, to_apply=%region_27.28.clone | all-reduce | flops 9216 | bytes 73728
  801.2 3.4 fusion.73
  807.2 3.2 add_add_fusion
  810.4 29.3 %reduce-scatter.23.cloned.1.call-done = f32[24,768]{1,0:T(8,128)} async-done(((f32[768,768]{1,0:T(8,128)}), f32[24,768]{1,0:T(8,128)}) %reduce-scatter.23.cloned.1.call-update) | async-done | bytes 73744
  839.7 104.4 %reduce-scatter.19.cloned.1.call-done = f32[24,768]{1,0:T(8,128)} async-done(((f32[768,768]{1,0:T(8,128)}), f32[24,768]{1,0:T(8,128)}) %reduce-scatter.19.cloned.1.call-update) | async-done | bytes 73744
  944.1 141.7 %reduce-scatter.15.cloned.1.call-done = f32[24,3072]{1,0:T(8,128)} async-done(((f32[768,3072]{1,0:T(8,128)}), f32[24,3072]{1,0:T(8,128)}) %reduce-scatter.15.cloned.1.call-update) | async-done | bytes 294928 | tf_op jit(solution)/shard_map/reduce_scatter | solution.py:306
  1085.8 141.5 %reduce-scatter.17.cloned.1.call-done = f32[96,768]{1,0:T(8,128)} async-done(((f32[3072,768]{1,0:T(8,128)}), f32[96,768]{1,0:T(8,128)}) %reduce-scatter.17.cloned.1.call-update) | async-done | bytes 294928 | tf_op jit(solution)/shard_map/reduce_scatter | solution.py:307
  (484 shorter events, 289.8 us)
Async XLA Ops:
  7.2 61.3 %all-gather.11.cloned.1.call-start = ((), (), s32[]{:S(2)}) async-start(), calls=%async_computation.16 | async-start | bytes 1216512 | tf_op jit(solution)/shard_map/all_gather | solution.py:172
  8.8 121.8 %all-gather.7.cloned.1.call-start = ((), (), s32[]{:S(2)}) async-start(), calls=%async_computation.14 | async-start | bytes 1216512 | tf_op jit(solution)/shard_map/all_gather | solution.py:170
  10.3 181.8 %all-gather.9.cloned.1.call-start = ((), (), s32[]{:S(2)}) async-start(), calls=%async_computation.15 | async-start | bytes 1216512 | tf_op jit(solution)/shard_map/all_gather | solution.py:171
  11.9 341.5 %all-gather.13.cloned.1.call-start = ((), (), s32[]{:S(2)}) async-start(), calls=%async_computation.17 | async-start | bytes 1216512 | tf_op jit(solution)/shard_map/all_gather | solution.py:173
  13.5 344.4 %all-gather.15.cloned.1.call-start = ((), (), s32[]{:S(2)}) async-start(), calls=%async_computation.18 | async-start | bytes 4866048 | tf_op jit(solution)/shard_map/all_gather | solution.py:174
  74.7 64.2 %all-to-all-start.2 = ((bf16[4,256,12,64]{1,0,3,2:T(4,128)(2,1)}), bf16[4,256,12,64]{1,0,3,2:T(4,128)(2,1)S(1)}, u32[]{:S(2)}, u32[]{:S(2)}) async-start(bf16[4,256,12,64]{1,0,3,2:T(4,128)(2,1)} %reshape.248), calls=%async_computation.2 | async-start | bytes 3145728 | tf_op jit(solution)/shard_map/all_to_all | solution.py:206
  138.9 64.1 %all-to-all-start = ((bf16[4,256,12,64]{1,0,3,2:T(4,128)(2,1)}), bf16[4,256,12,64]{1,0,3,2:T(4,128)(2,1)S(1)}, u32[]{:S(2)}, u32[]{:S(2)}) async-start(bf16[4,256,12,64]{1,0,3,2:T(4,128)(2,1)} %reshape.246), calls=%async_computation | async-start | bytes 3145728 | tf_op jit(solution)/shard_map/all_to_all | solution.py:202
  199.1 8.5 copy-start.24
  199.1 9.2 copy-start.39
  203.0 25.4 %all-to-all-start.1 = ((bf16[4,256,12,64]{1,0,3,2:T(4,128)(2,1)}), bf16[4,256,12,64]{1,0,3,2:T(4,128)(2,1)}, u32[]{:S(2)}, u32[]{:S(2)}) async-start(bf16[4,256,12,64]{1,0,3,2:T(4,128)(2,1)} %reshape.247), calls=%async_computation.1 | async-start | bytes 3145728 | tf_op jit(solution)/shard_map/all_to_all | solution.py:205
  207.3 177.4 %all-gather.17.cloned.1.call-start = ((), (), s32[]{:S(2)}) async-start(), calls=%async_computation.19 | async-start | bytes 4866048 | tf_op jit(solution)/shard_map/all_gather | solution.py:175
  304.5 8.5 copy-start.2
  313.0 10.0 copy-start.45
  313.0 10.0 copy-start.44
  313.0 10.0 copy-start.43
  313.0 10.0 copy-start.42
  313.0 10.0 copy-start.41
  313.0 10.1 copy-start.40
  313.0 10.1 copy-start.3
  318.3 6.1 copy-start.36
  318.3 24.6 %all-to-all-start.3 = ((bf16[4,2,98304]{2,1,0:T(2,128)(2,1)}), bf16[4,2,98304]{2,1,0:T(2,128)(2,1)}, u32[]{:S(2)}, u32[]{:S(2)}) async-start(bf16[4,2,98304]{2,1,0:T(2,128)(2,1)} %reshape.299), calls=%async_computation.3 | async-start | bytes 3145728 | tf_op jit(solution)/shard_map/all_to_all | solution.py:210
  323.0 97.3 %copy-start.27 = (f32[768]{0:T(1024)}, f32[768]{0:T(1024)S(1)}, u32[]{:S(2)}) copy-start(f32[768]{0:T(1024)S(1)} %convert_element_type.180) | copy-start | bytes 9220
  323.0 61.8 %copy-start.29 = (f32[768]{0:T(1024)}, f32[768]{0:T(1024)S(1)}, u32[]{:S(2)}) copy-start(f32[768]{0:T(1024)S(1)} %convert_element_type.182) | copy-start | bytes 9220
  357.3 63.0 %copy-start = (f32[1024,768]{1,0:T(8,128)}, f32[1024,768]{1,0:T(8,128)S(1)}, u32[]{:S(2)}) copy-start(f32[1024,768]{1,0:T(8,128)S(1)} %get-tuple-element.629) | copy-start | bytes 9437188
  357.4 63.0 %copy-start.22 = (f32[1024]{0:T(1024)}, f32[1024]{0:T(1024)S(1)}, u32[]{:S(2)}) copy-start(f32[1024]{0:T(1024)S(1)} %broadcast_multiply_fusion.4) | copy-start | bytes 12292
  357.9 62.5 %copy-start.25 = (f32[1024]{0:T(1024)}, f32[1024]{0:T(1024)S(1)}, u32[]{:S(2)}) copy-start(f32[1024]{0:T(1024)S(1)} %add_rsqrt_fusion.1) | copy-start | bytes 12292
  396.8 2.9 copy-start.46
  396.8 17.0 %slice-start = ((s8[4718592]{0:T(1024)(128)(4,1)}), s8[4194304]{0:T(1024)(128)(4,1)S(1)}, s32[]{:S(2)}) async-start(s8[4718592]{0:T(1024)(128)(4,1)} %bitcast.315), calls=%async_computation.26 | async-start | bytes 8388608
  399.7 14.1 %copy-start.16 = (f32[1024,768]{1,0:T(8,128)}, f32[1024,768]{1,0:T(8,128)S(1)}, u32[]{:S(2)}) copy-start(f32[1024,768]{1,0:T(8,128)S(1)} %get-tuple-element.612) | copy-start | bytes 9437188
  399.7 14.1 %slice-start.1 = ((s8[4718592]{0:T(1024)(128)(4,1)}), s8[524288]{0:T(1024)(128)(4,1)S(1)}, s32[]{:S(2)}) async-start(s8[4718592]{0:T(1024)(128)(4,1)} %bitcast.315), calls=%async_computation.27 | async-start | bytes 1048576
  413.8 6.5 copy-start.13
  420.4 3.4 copy-start.51
  422.1 1.7 copy-start.9
  426.9 8.4 copy-start.10
  430.9 24.4 %all-to-all-start.4 = ((bf16[4,256,12,64]{1,0,3,2:T(4,128)(2,1)}), bf16[4,256,12,64]{1,0,3,2:T(4,128)(2,1)}, u32[]{:S(2)}, u32[]{:S(2)}) async-start(bf16[4,256,12,64]{1,0,3,2:T(4,128)(2,1)} %reshape.251), calls=%async_computation.4 | async-start | bytes 3145728 | tf_op jit(solution)/shard_map/all_to_all | solution.py:255
  435.3 375.2 %reduce-scatter.13.cloned.1.call-start = ((), (), s32[]{:S(2)}) async-start(), calls=%async_computation.20 | async-start | bytes 2433024 | tf_op jit(solution)/shard_map/reduce_scatter | solution.py:305
  439.6 370.8 %reduce-scatter.21.cloned.1.call-start = ((), (), s32[]{:S(2)}) async-start(), calls=%async_computation.24 | async-start | bytes 2433024
  627.6 2.8 copy-start.47
  633.9 205.9 %reduce-scatter.23.cloned.1.call-start = ((), (), s32[]{:S(2)}) async-start(), calls=%async_computation.25 | async-start | bytes 2433024
  667.1 6.6 copy-start.48
  672.0 4.5 copy-start.5
  679.6 264.5 %reduce-scatter.19.cloned.1.call-start = ((), (), s32[]{:S(2)}) async-start(), calls=%async_computation.23 | async-start | bytes 2433024
  715.2 6.5 copy-start.49
  724.5 3.3 copy-start.1
  724.5 3.3 copy-start.23
  724.5 3.3 copy-start.26
  724.5 3.3 copy-start.28
  724.5 3.3 copy-start.30
  727.8 358.0 %reduce-scatter.15.cloned.1.call-start = ((), (), s32[]{:S(2)}) async-start(), calls=%async_computation.21 | async-start | bytes 9732096 | tf_op jit(solution)/shard_map/reduce_scatter | solution.py:306
  738.5 1.9 copy-start.17
  738.6 488.7 %reduce-scatter.17.cloned.1.call-start = ((), (), s32[]{:S(2)}) async-start(), calls=%async_computation.22 | async-start | bytes 9732096 | tf_op jit(solution)/shard_map/reduce_scatter | solution.py:307
  750.6 3.3 copy-start.8
  750.6 5.1 copy-start.31
  750.7 5.1 copy-start.32
  750.7 5.1 copy-start.33
  750.7 5.1 copy-start.34
  750.7 5.1 copy-start.35
  750.7 5.1 copy-start.37
  750.7 5.1 copy-start.38
  801.2 3.4 copy-start.20
  801.2 3.4 copy-start.50
  804.6 1.9 copy-start.11
  804.6 2.3 copy-start.15
  804.6 2.7 copy-start.21
  (10 other events, 10.9 us)
Sparse Core Ops, SparseCore 0:
  11.6 56.8 all-gather.10
  72.0 58.4 all-gather.6
  134.2 57.9 all-gather.8
  195.6 53.8 all-gather.12
  252.9 62.6 all-gather.14
  319.1 65.6 all-gather.16
  441.9 99.3 reduce-scatter.12
  634.0 100.7 reduce-scatter.20
  740.6 99.0 reduce-scatter.22
  845.4 98.6 reduce-scatter.18
  950.6 135.1 reduce-scatter.14
  1092.1 135.1 reduce-scatter.16
